TPU v7x, 32 devices: a whole 2x2x4 slice. The times are simulated.
32 devices in a mesh: row: 4 (over z), col: 4 (over y, x), walk: 2 (over core).
Axes of the slice: x: 2, y: 2, z: 4, core: 2. Of those that a mesh axis runs over, the one named last changes fastest.
Arguments:
- one_elec: bfloat16 [8, 512, 256], P('walk', ('row', 'col')), parts along dimension 0, may hold values from -13 to 13
- pair: bfloat16 [8, 512, 512, 128], P('walk', 'row', 'col'), parts along dimension 0, may hold values from -11 to 11
- spins: int32 [512], replicated, may hold values from 0 to 1, as said below
- w_single: bfloat16 [1024, 256], replicated, may hold values from -0.1875 to 0.1875
- b_single: float32 [256], replicated, may hold values from -1 to 1
- w_pair: bfloat16 [128, 128], replicated, may hold values from -0.5 to 0.5
- w_msg: bfloat16 [256, 128], replicated, may hold values from -0.375 to 0.375
- b_pair: float32 [128], replicated, may hold values from -1 to 1
- d_single: bfloat16 [8, 512, 256], P('walk', ('row', 'col')), parts along dimension 0, may hold values from -13 to 13
- d_pair: bfloat16 [8, 512, 512, 128], P('walk', 'row', 'col'), parts along dimension 0, may hold values from -6 to 6
Outputs:
- single_out: bfloat16 [8, 512, 256], P('walk', ('row', 'col')), parts along dimension 0
- pair_out: bfloat16 [8, 512, 512, 128], P('walk', 'row', 'col'), parts along dimension 0
- grad_single: float32 [8, 512, 256], P('walk', ('row', 'col')), parts along dimension 0
- grad_pair: bfloat16 [8, 512, 512, 128], P('walk', 'row', 'col'), parts along dimension 0
There are 2 independent parts, one for each index of `walk`. A program takes and returns all parts, laid end to end along the dimension named above; an argument that names none is the same for every part. Nothing has to cross between parts.
Inputs may be any that keep to these rules, and one draw needn't show every extreme that they name: `spins`: 1 marks a spin-up electron and 0 a spin-down one; from 128 to 384 electrons are up.
All inputs are finite; a program needn't handle non-finite values.
Results may differ from a plain program's by a relative error of at most 0.005.
Values may be sent and summed in bfloat16 or wider, within the bound.
No kernel may reach another device: no remote copies, remote signals or barrier semaphores. Data moves between devices by JAX's collectives and lax.ppermute only.
A program may use at most 192 MiB of HBM per device.

v0:
```python
import jax
import jax.numpy as jnp
from jax import lax
from jax.sharding import PartitionSpec as P

highest = lax.Precision.HIGHEST


def from_root(value, axis, source):
    kept = jnp.where(lax.axis_index(axis) == source, value, 0).astype(value.dtype)
    return lax.psum(kept, axis)


def body(one_elec, pair, spins, w_single, b_single, w_pair, w_msg, b_pair, d_single, d_pair):
    walkers, block_rows, block_cols, width_pair = pair.shape
    own_rows = one_elec.shape[1]
    width_single = one_elec.shape[2]
    electrons = spins.shape[0]
    pair_down = float(electrons) ** (-0.75)
    pair_boost = float(electrons) ** 0.75
    row_index = lax.axis_index("row")
    col_index = lax.axis_index("col")
    spin_up = spins.astype(jnp.float32)
    spin_down = 1.0 - spin_up
    count_up = jnp.sum(spin_up)
    count_down = jnp.sum(spin_down)
    counts = jnp.stack([count_up, count_down])
    spin_table = jnp.stack([spin_up, spin_down], axis=1)
    col_start = col_index * block_cols
    own_start = (row_index * lax.axis_size("col") + col_index) * own_rows
    col_table = lax.dynamic_slice_in_dim(spin_table, col_start, block_cols, 0)
    own_table = lax.dynamic_slice_in_dim(spin_table, own_start, own_rows, 0)
    everyone = lax.all_gather(one_elec, ("row", "col"), axis=1, tiled=True)
    spin_sums = jnp.einsum(
        "wjd,js->wsd", everyone, spin_table.astype(jnp.bfloat16), preferred_element_type=jnp.float32
    )
    col_single = lax.dynamic_slice_in_dim(everyone, col_start, block_cols, 1)
    spin_means = spin_sums / counts[None, :, None]
    partial_value = jnp.einsum(
        "wijd,js->wisd", pair, col_table.astype(jnp.bfloat16), preferred_element_type=jnp.float32
    )
    summed_pair = lax.psum(partial_value.astype(jnp.bfloat16), "col").astype(jnp.float32)
    own_sum = lax.dynamic_slice_in_dim(summed_pair, col_index * own_rows, own_rows, 1)
    pair_means = own_sum / counts[None, None, :, None]
    single_wide = one_elec.astype(jnp.float32)
    features = jnp.concatenate(
        [
            single_wide,
            jnp.broadcast_to(spin_means[:, None, 0, :], (walkers, own_rows, width_single)),
            jnp.broadcast_to(spin_means[:, None, 1, :], (walkers, own_rows, width_single)),
            pair_means[:, :, 0, :],
            pair_means[:, :, 1, :],
        ],
        axis=2,
    ).astype(jnp.bfloat16)
    single_act = jnp.tanh(
        jnp.einsum("wif,fd->wid", features, w_single, preferred_element_type=jnp.float32) + b_single
    )
    single_out = (single_wide + single_act).astype(jnp.bfloat16)
    message = jnp.einsum("wjd,de->wje", col_single, w_msg, preferred_element_type=jnp.float32)
    pre_pair = (
        jnp.einsum("wijd,de->wije", pair, w_pair, preferred_element_type=jnp.float32)
        + message[:, None, :, :]
        + b_pair
    )
    pair_act = jnp.tanh(pre_pair)
    pair_out = (pair.astype(jnp.float32) + pair_act).astype(jnp.bfloat16)
    grad_pre = (d_single.astype(jnp.float32) * (1.0 - single_act * single_act)).astype(jnp.bfloat16)
    feature_grad = jnp.einsum("wid,fd->wif", grad_pre, w_single, preferred_element_type=jnp.float32)
    grad_direct = feature_grad[:, :, :width_single]
    grad_means = feature_grad[:, :, width_single : 3 * width_single].reshape(
        walkers, own_rows, 2, width_single
    )
    grad_pair_means = feature_grad[:, :, 3 * width_single :].reshape(
        walkers, own_rows, 2, width_pair
    )
    row_pair_grads = lax.all_gather(
        grad_pair_means.astype(jnp.bfloat16), "col", axis=1, tiled=True
    ).astype(grad_pair_means.dtype)
    col_up = col_table[:, 0]
    col_down = col_table[:, 1]
    spread_pair = (
        col_up[None, None, :, None] * (row_pair_grads[:, :, 0, :] / count_up)[:, :, None, :]
        + col_down[None, None, :, None] * (row_pair_grads[:, :, 1, :] / count_down)[:, :, None, :]
    )
    pair_delta = (d_pair.astype(jnp.float32) * (1.0 - pair_act * pair_act)).astype(jnp.bfloat16)
    back_pair = jnp.einsum("wije,de->wijd", pair_delta, w_pair, preferred_element_type=jnp.float32)
    grad_pair = (d_pair.astype(jnp.float32) + back_pair + pair_boost * spread_pair).astype(
        jnp.bfloat16
    )
    column_sum = jnp.sum(pair_delta, axis=1, dtype=jnp.float32)
    message_grad = pair_down * jnp.einsum(
        "wje,de->wjd", column_sum, w_msg.astype(jnp.float32), precision=highest
    )
    mean_sums = jnp.sum(grad_means, axis=1)
    column_total = lax.psum(message_grad.astype(jnp.bfloat16), "row").astype(jnp.float32)
    row_total = from_root(column_total.astype(jnp.bfloat16), "col", row_index).astype(
        column_total.dtype
    )
    own_message = lax.dynamic_slice_in_dim(row_total, col_index * own_rows, own_rows, 1)
    mean_total = lax.psum(mean_sums, ("row", "col"))
    own_up = own_table[:, 0]
    own_down = own_table[:, 1]
    electron_grad = (
        own_up[None, :, None] * (mean_total[:, 0, :] / count_up)[:, None, :]
        + own_down[None, :, None] * (mean_total[:, 1, :] / count_down)[:, None, :]
        + own_message
    )
    grad_single = d_single.astype(jnp.float32) + grad_direct + electron_grad
    return (single_out, pair_out, grad_single, grad_pair)


def solution(mesh):
    placed = (
        P("walk", ("row", "col"), None),
        P("walk", "row", "col", None),
        P(),
        P(),
        P(),
        P(),
        P(),
        P(),
        P("walk", ("row", "col"), None),
        P("walk", "row", "col", None),
    )
    return jax.shard_map(
        body,
        mesh=mesh,
        in_specs=placed,
        out_specs=(
            P("walk", ("row", "col"), None),
            P("walk", "row", "col", None),
            P("walk", ("row", "col"), None),
            P("walk", "row", "col", None),
        ),
        check_vma=False,
    )
```

profile of v0, /device:TPU:0, one launch (start us, length us, event | category | flops | bytes accessed | tf_op | source)
XLA Modules:
  0.0 284.7 jit_solution(3167523664300797299)
XLA Ops:
  7.2 0.0 copy-start
  7.2 0.0 all-gather.2.cloned.1.call-start
  7.2 0.7 all-gather.2.cloned.1.call-update
  7.9 0.0 all-reduce.4.cloned.1.call-start
  8.0 0.7 convert_element_type.70
  8.7 1.4 convert_reduce_fusion.1
  10.0 1.3 pad_maximum_fusion.1
  11.3 0.1 fusion.32
  11.4 0.1 fusion.31
  11.5 0.8 constant_dynamic-update-slice_fusion
  12.4 8.8 %fusion.4 = bf16[4,128,2,128]{3,2,1,0:T(2,128)(2,1)} fusion(bf16[4,128,128,128]{3,2,1,0:T(8,128)(2,1)} %param.11, f32[128,2]{0,1:T(2,128)S(1)} %fusion.31), kind=kOutput, calls=%fused_computation.11 | convolution fusion | flops 33685760 | bytes 17040384 | tf_op jit(solution)/shard_map/wijd,js->wisd/dot_general | solution.py:39
  21.1 47.3 %all-gather.2.cloned.1.call-done = bf16[4,512,256]{2,1,0:T(8,128)(2,1)} async-done(((bf16[4,32,256]{2,1,0:T(8,128)(2,1)}), bf16[4,512,256]{2,1,0:T(8,128)(2,1)}) %all-gather.2.cloned.1.call-update) | async-done | bytes 1048592 | tf_op jit(solution)/shard_map/all_gather | solution.py:33
  68.4 1.2 fusion.12
  69.7 33.3 %add_convert_fusion = (bf16[4,128,128,128]{3,2,1,0:T(8,128)(2,1)}, f32[4,128,128]{2,1,0:T(8,128)S(1)}, f32[4,128,128,128]{3,2,1,0:T(8,128)}) fusion(bf16[4,128,128,128]{3,2,1,0:T(8,128)(2,1)} %param.11, f32[128]{0:T(128)} %param.17, f32[4,128,128]{2,1,0:T(8,128)S(1)} %fusion.12, bf16[4,128,128,128]{3,2,1,0:T(8,128)(2,1)} %param.19, bf16[128,128]{1,0:T(8,128)(2,1)} %param.15), kind=kOutput, calls=%fused_computation.6 | convolution fusion | flops 2248081408 | bytes 84443648 | tf_op jit(solution)/shard_map/wijd,de->wije/dot_general | solution.py:62
  102.9 1.1 fusion.3
  104.0 0.0 all-reduce.4.cloned.1.call-update
  104.1 0.0 all-reduce.6.cloned.1.call-start
  104.1 0.2 fusion.6
  104.4 34.3 %all-reduce.4.cloned.1.call-done = bf16[4,128,256]{2,1,0:T(8,128)(2,1)} async-done(((bf16[4,128,256]{2,1,0:T(8,128)(2,1)}), bf16[4,128,256]{2,1,0:T(8,128)(2,1)}) %all-reduce.4.cloned.1.call-update) | async-done | bytes 262160 | tf_op jit(solution)/shard_map/psum | solution.py:96
  138.7 1.7 broadcast_select_fusion
  140.4 0.0 all-reduce.6.cloned.1.call-update
  140.4 47.2 %all-reduce.6.cloned.1.call-done = (bf16[4,128,2,128]{3,2,1,0:T(2,128)(2,1)}, bf16[4,128,256]{2,1,0:T(8,128)(2,1)}) async-done(((bf16[4,128,2,128]{3,2,1,0:T(2,128)(2,1)}, bf16[4,128,256]{2,1,0:T(8,128)(2,1)}), (bf16[4,128,2,128]{3,2,1,0:T(2,128)(2,1)}, bf16[4,128,256]{2,1,0:T(8,128)(2,1)})) %all-reduce.6.cloned.1.call-update) | async-done | bytes 524304 | tf_op jit(solution)/shard_map/psum | solution.py:42
  187.6 1.0 fusion.16
  188.5 0.1 fusion.39
  188.7 0.9 add_convert_fusion.1
  189.6 0.3 fusion.7
  190.0 41.3 %psum.29 = f32[4,2,256]{2,0,1:T(4,128)S(1)} all-reduce(f32[4,2,256]{2,0,1:T(4,128)S(1)} %bitcast.78), channel_id=1, replica_groups=mesh['row'=4,'col'=4,'walk'=2] {'row','col'}, use_global_device_ids=true, to_apply=%region_4.0 | all-reduce | flops 2048 | bytes 16384 | tf_op jit(solution)/shard_map/psum | solution.py:101
  231.3 1.3 fusion.27
  232.5 7.7 %all_gather.7 = bf16[4,128,2,128]{3,1,0,2:T(8,128)(2,1)S(1)} all-gather(bf16[4,32,2,128]{3,1,0,2:T(8,128)(2,1)S(1)} %copy_bitcast_fusion), channel_id=1, replica_groups=mesh['row'=4,'col'=4,'walk'=2] {'col'}, dimensions={1}, use_global_device_ids=true | all-gather | bytes 327680 | tf_op jit(solution)/shard_map/all_gather | solution.py:77
  240.2 1.3 fusion.11
  241.6 1.6 fusion.15
  243.2 35.0 %fusion.2 = bf16[4,128,128,128]{3,2,1,0:T(8,128)(2,1)} fusion(bf16[4,128,128,128]{3,2,1,0:T(8,128)(2,1)} %param.19, f32[4,128,128]{2,1,0:T(8,128)S(1)} %get-tuple-element.11, f32[128]{0:T(128)S(1)} %get-tuple-element.20, f32[4,128,128]{2,1,0:T(8,128)S(1)} %get-tuple-element.10, f32[128]{0:T(128)S(1)} %get-tuple-element.19, ...), kind=kOutput, calls=%fused_computation.4 | convolution fusion | flops 2273312768 | bytes 67929600 | tf_op jit(solution)/shard_map/wije,de->wijd/dot_general | solution.py:87
  (26 shorter events, 0.2 us)
Async XLA Ops:
  7.2 181.5 %copy-start = (bf16[1024,256]{1,0:T(8,128)(2,1)S(1)}, bf16[1024,256]{1,0:T(8,128)(2,1)}, u32[]{:S(2)}) copy-start(bf16[1024,256]{1,0:T(8,128)(2,1)} %param.13) | copy-start | bytes 1572868
  7.2 61.2 %all-gather.2.cloned.1.call-start = ((), (), s32[]{:S(2)}) async-start(), calls=%async_computation | async-start | bytes 1114112 | tf_op jit(solution)/shard_map/all_gather | solution.py:33
  7.9 130.8 %all-reduce.4.cloned.1.call-start = ((), (), s32[]{:S(2)}) async-start(), calls=%async_computation.1 | async-start | bytes 524288 | tf_op jit(solution)/shard_map/psum | solution.py:96
  69.6 33.4 %copy-start.4 = (bf16[256,128]{1,0:T(8,128)(2,1)S(1)}, bf16[256,128]{1,0:T(8,128)(2,1)}, u32[]{:S(2)}) copy-start(bf16[256,128]{1,0:T(8,128)(2,1)} %param.16) | copy-start | bytes 196612
  69.6 34.5 %copy-start.1 = (bf16[4,512,256]{2,1,0:T(8,128)(2,1)S(1)}, bf16[4,512,256]{2,1,0:T(8,128)(2,1)}, u32[]{:S(2)}) copy-start(bf16[4,512,256]{2,1,0:T(8,128)(2,1)} %all-gather.2.cloned.1.call-done) | copy-start | bytes 3145732
  69.6 119.1 %copy-start.2 = (bf16[4,32,256]{2,1,0:T(8,128)(2,1)S(1)}, bf16[4,32,256]{2,1,0:T(8,128)(2,1)}, u32[]{:S(2)}) copy-start(bf16[4,32,256]{2,1,0:T(8,128)(2,1)} %param.10) | copy-start | bytes 196612
  69.6 119.1 %copy-start.5 = (f32[256]{0:T(256)S(1)}, f32[256]{0:T(256)}, u32[]{:S(2)}) copy-start(f32[256]{0:T(256)} %param.14) | copy-start | bytes 3076
  69.6 120.0 %copy-start.3 = (bf16[4,32,256]{2,1,0:T(8,128)(2,1)S(1)}, bf16[4,32,256]{2,1,0:T(8,128)(2,1)}, u32[]{:S(2)}) copy-start(bf16[4,32,256]{2,1,0:T(8,128)(2,1)} %param.18) | copy-start | bytes 196612
  69.6 173.5 %copy-start.6 = (bf16[128,128]{1,0:T(8,128)(2,1)S(1)}, bf16[128,128]{1,0:T(8,128)(2,1)}, u32[]{:S(2)}) copy-start(bf16[128,128]{1,0:T(8,128)(2,1)} %param.15) | copy-start | bytes 98308
  69.6 173.5 %copy-start.7 = (f32[128]{0:T(128)S(1)}, f32[128]{0:T(128)}, u32[]{:S(2)}) copy-start(f32[128]{0:T(128)} %param.17) | copy-start | bytes 1540
  104.1 83.5 %all-reduce.6.cloned.1.call-start = ((), (), s32[]{:S(2)}) async-start(), calls=%async_computation.2 | async-start | bytes 1048576 | tf_op jit(solution)/shard_map/psum | solution.py:42
Sparse Core Ops, SparseCore 0:
  10.7 57.6 all-gather.1
  104.2 34.4 all-reduce.3
  142.3 45.2 all-reduce.5
where the time goes:
time: 285 us
  waiting for transfers between devices  129 us (45%)
  matrix products  80.7 us (28%)
  blocking collectives  48.9 us (17%)
  between operations  14 us (5%)
  other arithmetic  10.4 us (4%)
    all_gather x1, waiting for transfers between devices, body(): everyone = lax.all_gather(one_elec, ('row', 'col'), axis=1, tiled=True)  47.3 us
    psum x1, waiting for transfers between devices, body(): lax.psum(partial_value.astype(jnp.bfloat16), 'col').astype(jnp.float32)  47.2 us
    psum x1, blocking collectives, body(): mean_total = lax.psum(mean_sums, ('row', 'col'))  41.3 us
    dot_general x1, matrix products, body(): jnp.einsum('wije,de->wijd', pair_delta, w_pair, preferred_element_type=jn...  35 us
    psum x1, waiting for transfers between devices, body(): lax.psum(message_grad.astype(jnp.bfloat16), 'row').astype(jnp.float32)  34.3 us
    dot_general x1, matrix products, body(): jnp.einsum('wijd,de->wije', pair, w_pair, preferred_element_type=jnp.floa...  33.3 us
    dot_general x1, matrix products, body(): jnp.einsum('wijd,js->wisd', pair, col_table.astype(jnp.bfloat16), preferr...  8.75 us
    all_gather x1, blocking collectives, body(): lax.all_gather(grad_pair_means.astype(jnp.bfloat16), 'col', axis=1, tiled...  7.66 us
  transfers between devices with their start and end apart: 3, of which 3 were waited for; matrix products, arithmetic and copies ran while one was open for 5% of the time, Pallas kernels for 0%

commit v1 on v0

--- a/solution.py
+++ b/solution.py
@@ -2,8 +2,10 @@
 import jax.numpy as jnp
 from jax import lax
 from jax.sharding import PartitionSpec as P
+from jax.lax import all_gather
 
 highest = lax.Precision.HIGHEST
+_carry_unit = lambda my_data: jnp.sum(all_gather(my_data, axis_name=("row", "col")), 0)
 
 
 def from_root(value, axis, source):
@@ -98,7 +100,7 @@
         column_total.dtype
     )
     own_message = lax.dynamic_slice_in_dim(row_total, col_index * own_rows, own_rows, 1)
-    mean_total = lax.psum(mean_sums, ("row", "col"))
+    mean_total = _carry_unit(mean_sums)
     own_up = own_table[:, 0]
     own_down = own_table[:, 1]
     electron_grad = (

time: 285 us -> 284 us (level)
    psum x1 -> x0, blocking collectives: 41.3 us -> none  [body(): mean_total = lax.psum(mean_sums, ('row', 'col'))]
    all_gather x0 -> x1, blocking collectives: none -> 40.4 us  [all_gather(my_data, axis_name=('row', 'col'))]
where the time goes in v1:
time: 284 us
  waiting for transfers between devices  129 us (45%)
  matrix products  80.7 us (28%)
  blocking collectives  48 us (17%)
  between operations  14 us (5%)
  other arithmetic  10.4 us (4%)
    all_gather x1, waiting for transfers between devices, body(): everyone = lax.all_gather(one_elec, ('row', 'col'), axis=1, tiled=True)  47.3 us
    psum x1, waiting for transfers between devices, body(): lax.psum(partial_value.astype(jnp.bfloat16), 'col').astype(jnp.float32)  47.2 us
    all_gather x1, blocking collectives, all_gather(my_data, axis_name=('row', 'col'))  40.4 us
    dot_general x1, matrix products, body(): jnp.einsum('wije,de->wijd', pair_delta, w_pair, preferred_element_type=jn...  35 us
    psum x1, waiting for transfers between devices, body(): lax.psum(message_grad.astype(jnp.bfloat16), 'row').astype(jnp.float32)  34.3 us
    dot_general x1, matrix products, body(): jnp.einsum('wijd,de->wije', pair, w_pair, preferred_element_type=jnp.floa...  33.3 us
    dot_general x1, matrix products, body(): jnp.einsum('wijd,js->wisd', pair, col_table.astype(jnp.bfloat16), preferr...  8.75 us
    all_gather x1, blocking collectives, body(): lax.all_gather(grad_pair_means.astype(jnp.bfloat16), 'col', axis=1, tiled...  7.66 us
  transfers between devices with their start and end apart: 3, of which 3 were waited for; matrix products, arithmetic and copies ran while one was open for 5% of the time, Pallas kernels for 0%

profile of v1, /device:TPU:0, one launch (start us, length us, event | category | flops | bytes accessed | tf_op | source)
XLA Modules:
  0.0 283.8 jit_solution(6116458091535966705)
XLA Ops:
  7.2 0.0 copy-start
  7.2 0.0 all-gather.2.cloned.1.call-start
  7.2 0.7 all-gather.2.cloned.1.call-update
  7.9 0.0 all-reduce.4.cloned.1.call-start
  8.0 0.7 convert_element_type.70
  8.7 1.4 convert_reduce_fusion.1
  10.0 1.3 pad_maximum_fusion.1
  11.3 0.1 fusion.32
  11.4 0.1 fusion.31
  11.5 0.8 constant_dynamic-update-slice_fusion
  12.4 8.8 %fusion.4 = bf16[4,128,2,128]{3,2,1,0:T(2,128)(2,1)} fusion(bf16[4,128,128,128]{3,2,1,0:T(8,128)(2,1)} %param.11, f32[128,2]{0,1:T(2,128)S(1)} %fusion.31), kind=kOutput, calls=%fused_computation.11 | convolution fusion | flops 33685760 | bytes 17040384 | tf_op jit(solution)/shard_map/wijd,js->wisd/dot_general | solution.py:41
  21.1 47.3 %all-gather.2.cloned.1.call-done = bf16[4,512,256]{2,1,0:T(8,128)(2,1)} async-done(((bf16[4,32,256]{2,1,0:T(8,128)(2,1)}), bf16[4,512,256]{2,1,0:T(8,128)(2,1)}) %all-gather.2.cloned.1.call-update) | async-done | bytes 1048592 | tf_op jit(solution)/shard_map/all_gather | solution.py:35
  68.4 1.2 fusion.12
  69.7 33.3 %add_convert_fusion = (bf16[4,128,128,128]{3,2,1,0:T(8,128)(2,1)}, f32[4,128,128]{2,1,0:T(8,128)S(1)}, f32[4,128,128,128]{3,2,1,0:T(8,128)}) fusion(bf16[4,128,128,128]{3,2,1,0:T(8,128)(2,1)} %param.11, f32[128]{0:T(128)} %param.17, f32[4,128,128]{2,1,0:T(8,128)S(1)} %fusion.12, bf16[4,128,128,128]{3,2,1,0:T(8,128)(2,1)} %param.19, bf16[128,128]{1,0:T(8,128)(2,1)} %param.15), kind=kOutput, calls=%fused_computation.6 | convolution fusion | flops 2248081408 | bytes 84443648 | tf_op jit(solution)/shard_map/wijd,de->wije/dot_general | solution.py:64
  102.9 1.1 fusion.3
  104.0 0.0 all-reduce.4.cloned.1.call-update
  104.1 0.0 all-reduce.6.cloned.1.call-start
  104.1 0.2 fusion.6
  104.4 34.3 %all-reduce.4.cloned.1.call-done = bf16[4,128,256]{2,1,0:T(8,128)(2,1)} async-done(((bf16[4,128,256]{2,1,0:T(8,128)(2,1)}), bf16[4,128,256]{2,1,0:T(8,128)(2,1)}) %all-reduce.4.cloned.1.call-update) | async-done | bytes 262160 | tf_op jit(solution)/shard_map/psum | solution.py:98
  138.7 1.7 broadcast_select_fusion
  140.4 0.0 all-reduce.6.cloned.1.call-update
  140.4 47.2 %all-reduce.6.cloned.1.call-done = (bf16[4,128,2,128]{3,2,1,0:T(2,128)(2,1)}, bf16[4,128,256]{2,1,0:T(8,128)(2,1)}) async-done(((bf16[4,128,2,128]{3,2,1,0:T(2,128)(2,1)}, bf16[4,128,256]{2,1,0:T(8,128)(2,1)}), (bf16[4,128,2,128]{3,2,1,0:T(2,128)(2,1)}, bf16[4,128,256]{2,1,0:T(8,128)(2,1)})) %all-reduce.6.cloned.1.call-update) | async-done | bytes 524304 | tf_op jit(solution)/shard_map/psum | solution.py:44
  187.6 1.0 fusion.16
  188.5 0.1 fusion.39
  188.7 0.9 add_convert_fusion.1
  189.6 0.3 fusion.7
  190.0 40.4 %all_gather.14 = f32[16,4,2,256]{3,1,2,0:T(4,128)S(1)} all-gather(f32[1,4,2,256]{3,1,2,0:T(4,128)S(1)} %bitcast.78), channel_id=1, replica_groups=mesh['row'=4,'col'=4,'walk'=2] {'row','col'}, dimensions={0}, use_global_device_ids=true | all-gather | bytes 139264 | tf_op jit(solution)/shard_map/all_gather | solution.py:8
  230.4 1.3 fusion.27
  231.6 7.7 %all_gather.15 = bf16[4,128,2,128]{3,1,0,2:T(8,128)(2,1)S(1)} all-gather(bf16[4,32,2,128]{3,1,0,2:T(8,128)(2,1)S(1)} %copy_bitcast_fusion), channel_id=1, replica_groups=mesh['row'=4,'col'=4,'walk'=2] {'col'}, dimensions={1}, use_global_device_ids=true | all-gather | bytes 327680 | tf_op jit(solution)/shard_map/all_gather | solution.py:79
  239.3 1.3 fusion.11
  240.7 1.6 fusion.15
  242.3 35.0 %fusion.2 = bf16[4,128,128,128]{3,2,1,0:T(8,128)(2,1)} fusion(bf16[4,128,128,128]{3,2,1,0:T(8,128)(2,1)} %param.19, f32[4,128,128]{2,1,0:T(8,128)S(1)} %get-tuple-element.11, f32[128]{0:T(128)S(1)} %get-tuple-element.20, f32[4,128,128]{2,1,0:T(8,128)S(1)} %get-tuple-element.10, f32[128]{0:T(128)S(1)} %get-tuple-element.19, ...), kind=kOutput, calls=%fused_computation.4 | convolution fusion | flops 2273312768 | bytes 67929600 | tf_op jit(solution)/shard_map/wije,de->wijd/dot_general | solution.py:89
  (27 shorter events, 0.2 us)
Async XLA Ops:
  7.2 181.5 %copy-start = (bf16[1024,256]{1,0:T(8,128)(2,1)S(1)}, bf16[1024,256]{1,0:T(8,128)(2,1)}, u32[]{:S(2)}) copy-start(bf16[1024,256]{1,0:T(8,128)(2,1)} %param.13) | copy-start | bytes 1572868
  7.2 61.2 %all-gather.2.cloned.1.call-start = ((), (), s32[]{:S(2)}) async-start(), calls=%async_computation | async-start | bytes 1114112 | tf_op jit(solution)/shard_map/all_gather | solution.py:35
  7.9 130.8 %all-reduce.4.cloned.1.call-start = ((), (), s32[]{:S(2)}) async-start(), calls=%async_computation.1 | async-start | bytes 524288 | tf_op jit(solution)/shard_map/psum | solution.py:98
  69.6 33.4 %copy-start.4 = (bf16[256,128]{1,0:T(8,128)(2,1)S(1)}, bf16[256,128]{1,0:T(8,128)(2,1)}, u32[]{:S(2)}) copy-start(bf16[256,128]{1,0:T(8,128)(2,1)} %param.16) | copy-start | bytes 196612
  69.6 34.5 %copy-start.1 = (bf16[4,512,256]{2,1,0:T(8,128)(2,1)S(1)}, bf16[4,512,256]{2,1,0:T(8,128)(2,1)}, u32[]{:S(2)}) copy-start(bf16[4,512,256]{2,1,0:T(8,128)(2,1)} %all-gather.2.cloned.1.call-done) | copy-start | bytes 3145732
  69.6 119.1 %copy-start.2 = (bf16[4,32,256]{2,1,0:T(8,128)(2,1)S(1)}, bf16[4,32,256]{2,1,0:T(8,128)(2,1)}, u32[]{:S(2)}) copy-start(bf16[4,32,256]{2,1,0:T(8,128)(2,1)} %param.10) | copy-start | bytes 196612
  69.6 119.1 %copy-start.5 = (f32[256]{0:T(256)S(1)}, f32[256]{0:T(256)}, u32[]{:S(2)}) copy-start(f32[256]{0:T(256)} %param.14) | copy-start | bytes 3076
  69.6 120.0 %copy-start.3 = (bf16[4,32,256]{2,1,0:T(8,128)(2,1)S(1)}, bf16[4,32,256]{2,1,0:T(8,128)(2,1)}, u32[]{:S(2)}) copy-start(bf16[4,32,256]{2,1,0:T(8,128)(2,1)} %param.18) | copy-start | bytes 196612
  69.6 172.6 %copy-start.6 = (bf16[128,128]{1,0:T(8,128)(2,1)S(1)}, bf16[128,128]{1,0:T(8,128)(2,1)}, u32[]{:S(2)}) copy-start(bf16[128,128]{1,0:T(8,128)(2,1)} %param.15) | copy-start | bytes 98308
  69.6 172.6 %copy-start.7 = (f32[128]{0:T(128)S(1)}, f32[128]{0:T(128)}, u32[]{:S(2)}) copy-start(f32[128]{0:T(128)} %param.17) | copy-start | bytes 1540
  104.1 83.5 %all-reduce.6.cloned.1.call-start = ((), (), s32[]{:S(2)}) async-start(), calls=%async_computation.2 | async-start | bytes 1048576 | tf_op jit(solution)/shard_map/psum | solution.py:44
Sparse Core Ops, SparseCore 0:
  10.7 57.6 all-gather.1
  104.2 34.4 all-reduce.3
  142.3 45.2 all-reduce.5
